TPU v7x, 256 devices: a whole 4x4x8 slice. The times are simulated.
256 devices in a mesh: blk: 32 (over x_lo, z, core), tp: 8 (over y, x_hi).
Axes of the slice: x: 4 (x_hi: 2, x_lo: 2; x = x_hi * 2 + x_lo), y: 4, z: 8, core: 2. Of those that a mesh axis runs over, the one named last changes fastest.
Arguments:
- hidden_in: bfloat16 [12288, 4096], P('blk'), may hold values from -6 to 6
- w_query: bfloat16 [4096, 4096], P('blk', 'tp'), may hold values from -0.09375 to 0.09375
- w_key: bfloat16 [4096, 1024], P('blk', 'tp'), may hold values from -0.09375 to 0.09375
- w_value: bfloat16 [4096, 1024], P('blk', 'tp'), may hold values from -0.09375 to 0.09375
- starts: int32 [32], P('blk'), may hold values from 0 to 1152, as said below
- key_cache: bfloat16 [32, 1152, 1024], P('blk', None, 'tp'), may hold values from -400 to 400
- value_cache: bfloat16 [32, 1152, 1024], P('blk', None, 'tp'), may hold values from -6 to 6
- grad_out: bfloat16 [12288, 4096], P('blk', 'tp'), may hold values from -6 to 6
Outputs:
- attended: bfloat16 [12288, 4096], P('blk', 'tp')
- grad_in: bfloat16 [12288, 4096], P('blk', 'tp')
- grad_wq: float32 [4096, 4096], P('blk', 'tp')
- grad_wk: float32 [4096, 1024], P('blk', 'tp')
- grad_wv: float32 [4096, 1024], P('blk', 'tp')
Inputs may be any that keep to these rules, and one draw needn't show every extreme that they name: `starts`: every entry is a multiple of 384; both 0 and 1152 occur.
All inputs are finite; a program needn't handle non-finite values.
Results may differ from a plain program's by a relative error of at most 0.025.
The roundings to bfloat16 on the way count: a program that leaves them out, or rounds other values in their place, can miss the bound.
Values may be sent and summed in bfloat16 or wider, within the bound.
No kernel may reach another device: no remote copies, remote signals or barrier semaphores. Data moves between devices by JAX's collectives and lax.ppermute only.
A program may use at most 128 MiB of HBM per device.

v0:
```python
import jax
import jax.numpy as jnp
from jax import lax
from jax.sharding import PartitionSpec as P

H = 32
KV = 8
HD = 128


def contract_last(left, right):
    return lax.dot_general(
        left, right, (((1,), (1,)), ((), ())), preferred_element_type=jnp.float32
    )


def contract_first(left, right):
    return lax.dot_general(
        left, right, (((0,), (0,)), ((), ())), preferred_element_type=jnp.float32
    )


def head_pass(queries, cache_keys, cache_values, fresh_keys, fresh_values, grad_heads, offset):
    groups, row_count, head_width = queries.shape
    cached = cache_keys.shape[0]
    factor = head_width ** (-0.5)
    key_list = jnp.concatenate([cache_keys, fresh_keys], 0)
    value_list = jnp.concatenate([cache_values, fresh_values], 0)
    flat_query = queries.reshape(groups * row_count, head_width)
    flat_grad = grad_heads.reshape(groups * row_count, head_width)
    scores = contract_last(flat_query, key_list) * factor
    scores = scores.reshape(groups, row_count, cached + row_count)
    row_pos = lax.iota(jnp.int32, row_count)
    cache_ok = jnp.broadcast_to(lax.iota(jnp.int32, cached)[None, :] < offset, (row_count, cached))
    own_ok = row_pos[None, :] <= row_pos[:, None]
    allowed = jnp.concatenate([cache_ok, own_ok], 1)
    scores = jnp.where(allowed[None], scores, -jnp.inf)
    row_max = jnp.max(scores, axis=-1, keepdims=True)
    expo = jnp.exp(scores - row_max)
    probs = (expo / jnp.sum(expo, axis=-1, keepdims=True)).astype(jnp.bfloat16)
    probs = probs.reshape(groups * row_count, cached + row_count)
    attended = jnp.dot(probs, value_list, preferred_element_type=jnp.float32).astype(jnp.bfloat16)
    grad_probs = contract_last(flat_grad, value_list)
    probs_wide = probs.astype(jnp.float32)
    row_dot = jnp.sum(probs_wide * grad_probs, axis=-1, keepdims=True)
    grad_scores = (probs_wide * (grad_probs - row_dot) * factor).astype(jnp.bfloat16)
    grad_query = jnp.dot(grad_scores, key_list, preferred_element_type=jnp.float32).astype(
        jnp.bfloat16
    )
    grad_keys = contract_first(grad_scores[:, cached:], flat_query).astype(jnp.bfloat16)
    grad_values = contract_first(probs[:, cached:], flat_grad).astype(jnp.bfloat16)
    return (
        attended.reshape(groups, row_count, head_width),
        grad_query.reshape(groups, row_count, head_width),
        grad_keys,
        grad_values,
    )


def local(hidden_in, w_query, w_key, w_value, starts, key_cache, value_cache, grad_out):
    tokens_dev = hidden_in.shape[0]
    kv_local = w_key.shape[1] // HD
    group = H // KV
    cached = key_cache.shape[1]
    full_query, full_key, full_value = (
        lax.all_gather(w_query, "blk", axis=0, tiled=True),
        lax.all_gather(w_key, "blk", axis=0, tiled=True),
        lax.all_gather(w_value, "blk", axis=0, tiled=True),
    )
    proj_query = jnp.dot(hidden_in, full_query, preferred_element_type=jnp.float32)
    proj_key = jnp.dot(hidden_in, full_key, preferred_element_type=jnp.float32)
    proj_value = jnp.dot(hidden_in, full_value, preferred_element_type=jnp.float32)
    queries = proj_query.astype(jnp.bfloat16)
    new_keys = proj_key.astype(jnp.bfloat16)
    new_values = proj_value.astype(jnp.bfloat16)
    per_query = queries.reshape(tokens_dev, kv_local, group, HD).transpose(1, 2, 0, 3)
    per_grad = grad_out.reshape(tokens_dev, kv_local, group, HD).transpose(1, 2, 0, 3)
    cache_k = key_cache[0].reshape(cached, kv_local, HD).transpose(1, 0, 2)
    cache_v = value_cache[0].reshape(cached, kv_local, HD).transpose(1, 0, 2)
    fresh_k = new_keys.reshape(tokens_dev, kv_local, HD).transpose(1, 0, 2)
    fresh_v = new_values.reshape(tokens_dev, kv_local, HD).transpose(1, 0, 2)
    offset = starts[0]
    results = lax.map(
        lambda packed: head_pass(*packed, offset),
        (per_query, cache_k, cache_v, fresh_k, fresh_v, per_grad),
    )
    attended = results[0].transpose(2, 0, 1, 3).reshape(tokens_dev, kv_local * group * HD)
    grad_query = results[1].transpose(2, 0, 1, 3).reshape(tokens_dev, kv_local * group * HD)
    grad_keys = results[2].transpose(1, 0, 2).reshape(tokens_dev, kv_local * HD)
    grad_values = results[3].transpose(1, 0, 2).reshape(tokens_dev, kv_local * HD)
    input_term = (
        contract_last(grad_query, full_query)
        + contract_last(grad_keys, full_key)
        + contract_last(grad_values, full_value)
    )
    grad_in = lax.psum_scatter(input_term, "tp", scatter_dimension=1, tiled=True).astype(
        jnp.bfloat16
    )
    grads_cat = jnp.concatenate([grad_query, grad_keys, grad_values], 1)
    blk_count = lax.axis_size("blk")
    summed = lax.psum_scatter(
        contract_first(hidden_in, grads_cat), "blk", scatter_dimension=0, tiled=True
    )
    summed = summed * (tokens_dev * blk_count) ** (-0.5)
    query_cols = w_query.shape[1]
    kv_cols = w_key.shape[1]
    grad_wq = summed[:, :query_cols]
    grad_wk = summed[:, query_cols : query_cols + kv_cols]
    grad_wv = summed[:, query_cols + kv_cols :]
    return (attended, grad_in, grad_wq, grad_wk, grad_wv)


def solution(mesh):
    in_specs = (
        P("blk", None),
        P("blk", "tp"),
        P("blk", "tp"),
        P("blk", "tp"),
        P("blk"),
        P("blk", None, "tp"),
        P("blk", None, "tp"),
        P("blk", "tp"),
    )
    out_specs = (P("blk", "tp"), P("blk", "tp"), P("blk", "tp"), P("blk", "tp"), P("blk", "tp"))
    return jax.shard_map(local, mesh=mesh, in_specs=in_specs, out_specs=out_specs, check_vma=False)
```

profile of v0, /device:TPU:16, one launch (start us, length us, event | category | flops | bytes accessed | tf_op | source)
XLA Modules:
  0.0 504.6 jit_solution(6510871509543316294)
XLA Ops:
  7.2 0.0 copy-start
  7.2 0.0 all-gather.8.cloned.1.call-start
  7.2 0.7 all-gather.8.cloned.1.call-update
  7.9 0.0 all-gather.6.cloned.1.call-start
  8.0 0.7 all-gather.6.cloned.1.call-update
  8.7 0.0 all-gather.4.cloned.1.call-start
  8.7 0.7 all-gather.4.cloned.1.call-update
  9.4 0.0 reduce-scatter.3.cloned.1.call-start
  10.1 1.2 copy.27
  11.3 0.9 copy.28
  12.3 0.3 pad_add_fusion
  12.6 2.2 broadcast_in_dim.55
  14.8 2.6 copy.33
  17.4 58.8 %all-gather.8.cloned.1.call-done = bf16[4096,128]{1,0:T(8,128)(2,1)} async-done(((bf16[128,128]{1,0:T(8,128)(2,1)}), bf16[4096,128]{1,0:T(8,128)(2,1)}) %all-gather.8.cloned.1.call-update) | async-done | bytes 1048592 | tf_op jit(solution)/shard_map/all_gather | solution.py:68
  76.2 0.0 copy-done
  76.2 2.8 convolution_convert_fusion.3
  79.0 62.3 %all-gather.6.cloned.1.call-done = bf16[4096,128]{1,0:T(8,128)(2,1)} async-done(((bf16[128,128]{1,0:T(8,128)(2,1)}), bf16[4096,128]{1,0:T(8,128)(2,1)}) %all-gather.6.cloned.1.call-update) | async-done | bytes 1048592 | tf_op jit(solution)/shard_map/all_gather | solution.py:67
  141.3 2.8 convolution_convert_fusion.4
  144.2 65.3 %all-gather.4.cloned.1.call-done = bf16[4096,512]{1,0:T(8,128)(2,1)} async-done(((bf16[128,512]{1,0:T(8,128)(2,1)}), bf16[4096,512]{1,0:T(8,128)(2,1)}) %all-gather.4.cloned.1.call-update) | async-done | bytes 4194320 | tf_op jit(solution)/shard_map/all_gather | solution.py:66
  209.5 4.7 convolution_convert_fusion.2
  214.2 1.1 reshape.70
  215.3 0.1 copy.25
  215.4 3.6 fusion.27
  218.9 0.0 copy-start.6
  218.9 0.0 copy-start.7
  218.9 0.0 copy-start.11
  219.0 1.3 fusion.4
  220.3 0.0 copy-done.6
  220.3 0.0 copy-done.7
  220.3 0.0 copy-done.11
  220.3 5.0 fusion.1
  225.4 1.5 fusion.12
  226.9 8.0 %fusion.3 = bf16[1536,1536]{0,1:T(8,128)(2,1)} fusion(bf16[1536,1536]{0,1:T(8,128)(2,1)S(1)} %get-tuple-element.57, f32[1536,1536]{1,0:T(8,128)} %get-tuple-element.62, f32[1536]{0:T(1024)S(1)} %get-tuple-element.56), kind=kLoop, calls=%fused_computation.6 | loop fusion | flops 11796480 | bytes 18880512 | tf_op jit(solution)/shard_map/while/body/eval_jaxpr/convert_element_type | solution.py:46
  234.9 0.0 copy-done.1
  234.9 2.4 fusion.9
  237.3 0.0 copy-done.9
  237.3 0.0 copy-done.10
  237.3 4.5 convolution_convert_fusion
  241.8 1.2 copy.29
  243.1 0.0 copy-start.3
  243.1 0.0 copy-start.4
  243.1 4.1 fusion.28
  247.2 0.0 copy-done.3
  247.2 0.0 copy-done.4
  247.2 0.0 copy-start.2
  247.3 1.0 fusion.29
  248.3 0.2 copy-done.2
  248.5 3.7 add_add_fusion
  252.2 0.0 reduce-scatter.3.cloned.1.call-update
  252.2 0.0 reduce-scatter.5.cloned.1.call-start
  252.3 7.3 %convolution_bitcast_fusion = f32[4096,768]{0,1:T(8,128)} fusion(bf16[384,4096]{1,0:T(8,128)(2,1)S(1)} %copy-done, bf16[384,128]{0,1:T(8,128)(2,1)} %fusion.12, bf16[384,128]{0,1:T(8,128)(2,1)} %fusion.9, bf16[384,512]{0,1:T(8,128)(2,1)S(1)} %bitcast.56), kind=kOutput, calls=%fused_computation.11 | convolution fusion | flops 2417688576 | bytes 16318464 | tf_op jit(solution)/shard_map/dot_general | solution.py:18
  259.6 0.0 reduce-scatter.5.cloned.1.call-update
  259.6 0.9 copy-done.8
  260.5 0.1 copy-done.12
  260.6 3.8 convolution_convert_fusion.1
  264.3 0.3 copy.26
  264.7 0.8 copy.36
  265.5 88.7 %reduce-scatter.3.cloned.1.call-done = f32[384,512]{1,0:T(8,128)} async-done(((f32[384,4096]{1,0:T(8,128)}), f32[384,512]{1,0:T(8,128)}) %reduce-scatter.3.cloned.1.call-update) | async-done | bytes 786448 | tf_op jit(solution)/shard_map/reduce_scatter | solution.py:96
  354.2 1.9 convert_element_type.51
  356.1 138.6 %reduce-scatter.5.cloned.1.call-done = f32[128,768]{0,1:T(8,128)} async-done(((f32[4096,768]{0,1:T(8,128)}), f32[128,768]{0,1:T(8,128)}) %reduce-scatter.5.cloned.1.call-update) | async-done | bytes 393232 | tf_op jit(solution)/shard_map/reduce_scatter | solution.py:101
  494.7 1.0 broadcast_multiply_fusion
  495.8 0.8 copy.30
  496.6 0.7 copy.32
  497.3 0.7 copy.31
  (12 shorter events, 0.1 us)
Async XLA Ops:
  7.2 69.0 %copy-start = (bf16[384,4096]{1,0:T(8,128)(2,1)S(1)}, bf16[384,4096]{1,0:T(8,128)(2,1)}, u32[]{:S(2)}) copy-start(bf16[384,4096]{1,0:T(8,128)(2,1)} %param.8) | copy-start | bytes 9437188
  7.2 69.0 %all-gather.8.cloned.1.call-start = ((), (), s32[]{:S(2)}) async-start(), calls=%async_computation.4 | async-start | bytes 1081344 | tf_op jit(solution)/shard_map/all_gather | solution.py:68
  7.9 133.4 %all-gather.6.cloned.1.call-start = ((), (), s32[]{:S(2)}) async-start(), calls=%async_computation.3 | async-start | bytes 1081344 | tf_op jit(solution)/shard_map/all_gather | solution.py:67
  8.7 200.8 %all-gather.4.cloned.1.call-start = ((), (), s32[]{:S(2)}) async-start(), calls=%async_computation.2 | async-start | bytes 4325376 | tf_op jit(solution)/shard_map/all_gather | solution.py:66
  9.4 344.8 %reduce-scatter.3.cloned.1.call-start = ((), (), s32[]{:S(2)}) async-start(), calls=%async_computation.5 | async-start | bytes 7077888 | tf_op jit(solution)/shard_map/reduce_scatter | solution.py:96
  218.9 1.4 copy-start.6
  218.9 1.4 copy-start.7
  218.9 1.4 copy-start.11
  225.4 9.6 %copy-start.1 = (bf16[1536,1536]{0,1:T(8,128)(2,1)}, bf16[1536,1536]{0,1:T(8,128)(2,1)S(1)}, u32[]{:S(2)}) copy-start(bf16[1536,1536]{0,1:T(8,128)(2,1)S(1)} %get-tuple-element.57) | copy-start | bytes 14155780
  226.9 10.4 %copy-start.9 = (bf16[384,128]{1,0:T(8,128)(2,1)S(1)}, bf16[384,128]{1,0:T(8,128)(2,1)}, u32[]{:S(2)}) copy-start(bf16[384,128]{1,0:T(8,128)(2,1)} %convolution_convert_fusion.4) | copy-start | bytes 294916
  226.9 10.4 %copy-start.10 = (bf16[1,1152,128]{2,1,0:T(8,128)(2,1)S(1)}, bf16[1,1152,128]{2,1,0:T(8,128)(2,1)}, u32[]{:S(2)}) copy-start(bf16[1,1152,128]{2,1,0:T(8,128)(2,1)} %param.13) | copy-start | bytes 884740
  243.1 4.2 copy-start.3
  243.1 4.2 copy-start.4
  247.2 1.2 copy-start.2
  247.2 1.2 copy-start.5
  252.2 242.5 %reduce-scatter.5.cloned.1.call-start = ((), (), s32[]{:S(2)}) async-start(), calls=%async_computation.6 | async-start | bytes 12976128 | tf_op jit(solution)/shard_map/reduce_scatter | solution.py:101
  259.6 0.9 copy-start.8
  259.6 1.0 copy-start.12
Sparse Core Ops, SparseCore 0:
  9.8 66.3 all-gather.7
  78.0 63.2 all-gather.5
  143.2 66.2 all-gather.3
  252.3 101.7 reduce-scatter.2
  356.6 138.0 reduce-scatter.4
where the time goes:
time: 505 us
  waiting for transfers between devices  416 us (82%)
  matrix products  47.4 us (9%)
  between operations  14.6 us (3%)
  local copies, waits for them, and re-layouts  14 us (3%)
  other arithmetic  12.6 us (2%)
    reduce_scatter x1, waiting for transfers between devices, local(): lax.psum_scatter(contract_first(hidden_in, grads_cat), 'blk', scatter_dim...  139 us
    reduce_scatter x1, waiting for transfers between devices, local(): lax.psum_scatter(input_term, 'tp', scatter_dimension=1, tiled=True)  88.7 us
    all_gather x1, waiting for transfers between devices, local(): lax.all_gather(w_query, 'blk', axis=0, tiled=True)  65.3 us
    all_gather x1, waiting for transfers between devices, local(): lax.all_gather(w_key, 'blk', axis=0, tiled=True)  62.3 us
    all_gather x1, waiting for transfers between devices, local(): lax.all_gather(w_value, 'blk', axis=0, tiled=True)  58.8 us
    dot_general x5, matrix products, contract_last(): lax.dot_general(left, right, (((1,), (1,)), ((), ())), preferred_element_...  17.5 us
    dot_general x3, matrix products, contract_first(): lax.dot_general(left, right, (((0,), (0,)), ((), ())), preferred_element_...  11.3 us
  transfers between devices with their start and end apart: 5, of which 5 were waited for; matrix products, arithmetic and copies ran while one was open for 5% of the time, Pallas kernels for 0%

commit v1 on v0

--- a/solution.py
+++ b/solution.py
@@ -6,6 +6,13 @@
 H = 32
 KV = 8
 HD = 128
+
+
+def swapped_in(x, mesh_axis, d):
+    size = lax.axis_size(mesh_axis)
+    blocks = jnp.stack([x for _ in range(size)])
+    blocks = lax.all_to_all(blocks, mesh_axis, split_axis=0, concat_axis=0)
+    return jnp.concatenate(blocks, axis=d)
 
 
 def contract_last(left, right):
@@ -63,7 +70,7 @@
     group = H // KV
     cached = key_cache.shape[1]
     full_query, full_key, full_value = (
-        lax.all_gather(w_query, "blk", axis=0, tiled=True),
+        swapped_in(w_query, "blk", 0),
         lax.all_gather(w_key, "blk", axis=0, tiled=True),
         lax.all_gather(w_value, "blk", axis=0, tiled=True),
     )

time: 505 us -> 463 us (0.917)
  waiting for transfers between devices: 416 us -> 360 us
  starting transfers between devices: 0.19 us -> 10.1 us
    all_gather x1 -> x0, waiting for transfers between devices: 65.3 us -> none  [local(): lax.all_gather(w_query, 'blk', axis=0, tiled=True)]
    all_to_all x0 -> x1, starting transfers between devices: none -> 9.91 us  [swapped_in(): blocks = lax.all_to_all(blocks, mesh_axis, split_axis=0, concat_axis=0)]
    all_gather x1, waiting for transfers between devices: 58.8 us -> 66.7 us  [local(): lax.all_gather(w_value, 'blk', axis=0, tiled=True)]
  transfers between devices with their start and end apart: 5 -> 5, of which waited for: 5 -> 4; matrix products, arithmetic and copies ran while one was open for 5% -> 6% of each run, Pallas kernels for 0% -> 0%
where the time goes in v1:
time: 463 us; the launch traced here: 462 us
  waiting for transfers between devices  360 us (78%)
  matrix products  47.4 us (10%)
  local copies, waits for them, and re-layouts  17.5 us (4%)
  between operations  14.6 us (3%)
  other arithmetic  12.6 us (3%)
  starting transfers between devices  10.1 us (2%)
    reduce_scatter x1, waiting for transfers between devices, local(): lax.psum_scatter(contract_first(hidden_in, grads_cat), 'blk', scatter_dim...  138 us
    reduce_scatter x1, waiting for transfers between devices, local(): lax.psum_scatter(input_term, 'tp', scatter_dimension=1, tiled=True)  88.3 us
    all_gather x1, waiting for transfers between devices, local(): lax.all_gather(w_value, 'blk', axis=0, tiled=True)  66.7 us
    all_gather x1, waiting for transfers between devices, local(): lax.all_gather(w_key, 'blk', axis=0, tiled=True)  65.7 us
    dot_general x5, matrix products, contract_last(): lax.dot_general(left, right, (((1,), (1,)), ((), ())), preferred_element_...  17.5 us
    dot_general x3, matrix products, contract_first(): lax.dot_general(left, right, (((0,), (0,)), ((), ())), preferred_element_...  11.2 us
    all_to_all x1, starting transfers between devices, swapped_in(): blocks = lax.all_to_all(blocks, mesh_axis, split_axis=0, concat_axis=0)  9.91 us
  transfers between devices with their start and end apart: 5, of which 4 were waited for; matrix products, arithmetic and copies ran while one was open for 6% of the time, Pallas kernels for 0%

profile of v1, /device:TPU:16, one launch (start us, length us, event | category | flops | bytes accessed | tf_op | source)
XLA Modules:
  0.0 462.5 jit_solution(9318687529128566444)
XLA Ops:
  7.2 0.0 copy-start
  7.2 3.5 stack.2
  10.7 9.9 %all-to-all-start = ((bf16[32,128,512]{2,1,0:T(8,128)(2,1)}), bf16[32,128,512]{2,1,0:T(8,128)(2,1)}, u32[]{:S(2)}, u32[]{:S(2)}) async-start(bf16[32,128,512]{2,1,0:T(8,128)(2,1)} %stack.2), calls=%async_computation | async-start | bytes 8388608 | tf_op jit(solution)/shard_map/all_to_all | solution.py:14
  20.6 0.0 all-gather.5.cloned.1.call-start
  20.6 0.7 all-gather.5.cloned.1.call-update
  21.3 0.0 all-gather.3.cloned.1.call-start
  21.4 0.7 all-gather.3.cloned.1.call-update
  22.1 0.0 reduce-scatter.3.cloned.1.call-start
  22.7 1.2 copy.27
  24.0 0.9 copy.28
  25.0 0.3 pad_add_fusion
  25.3 2.2 broadcast_in_dim.55
  27.5 2.7 copy.33
  30.1 66.7 %all-gather.5.cloned.1.call-done = bf16[4096,128]{1,0:T(8,128)(2,1)} async-done(((bf16[128,128]{1,0:T(8,128)(2,1)}), bf16[4096,128]{1,0:T(8,128)(2,1)}) %all-gather.5.cloned.1.call-update) | async-done | bytes 1048592 | tf_op jit(solution)/shard_map/all_gather | solution.py:75
  96.8 0.0 copy-done
  96.8 2.8 convolution_convert_fusion.3
  99.7 65.7 %all-gather.3.cloned.1.call-done = bf16[4096,128]{1,0:T(8,128)(2,1)} async-done(((bf16[128,128]{1,0:T(8,128)(2,1)}), bf16[4096,128]{1,0:T(8,128)(2,1)}) %all-gather.3.cloned.1.call-update) | async-done | bytes 1048592 | tf_op jit(solution)/shard_map/all_gather | solution.py:74
  165.4 2.8 convolution_convert_fusion.4
  168.2 0.0 all-to-all-done
  168.2 4.7 %convolution_convert_fusion.2 = bf16[384,512]{1,0:T(8,128)(2,1)} fusion(bf16[384,4096]{1,0:T(8,128)(2,1)S(1)} %copy-done, bf16[4096,512]{1,0:T(8,128)(2,1)} %bitcast.1), kind=kOutput, calls=%fused_computation.16 | convolution fusion | flops 1610809344 | bytes 7733248 | tf_op jit(solution)/shard_map/dot_general | solution.py:77
  172.9 1.1 reshape.76
  174.0 0.1 copy.25
  174.1 3.6 fusion.27
  177.7 0.0 copy-start.6
  177.7 0.0 copy-start.7
  177.7 0.0 copy-start.11
  177.7 1.3 fusion.4
  179.0 0.0 copy-done.6
  179.0 0.0 copy-done.7
  179.0 0.0 copy-done.11
  179.0 5.0 %fusion.1 = (f32[1536]{0:T(1024)S(1)}, bf16[1536,1536]{0,1:T(8,128)(2,1)S(1)}, f32[1536,1536]{1,0:T(8,128)}) fusion(f32[1536]{0:T(1024)S(1)} %fusion.4, f32[1536,1536]{0,1:T(8,128)S(1)} %get-tuple-element.61, f32[1536]{0:T(1024)S(1)} %get-tuple-element.60, bf16[1536,128]{1,0:T(8,128)(2,1)S(1)} %bitcast.61, bf16[384,128]{1,0:T(8,128)(2,1)S(1)} %copy-done.7, ...), kind=kOutput, calls=%fused_computation.4 | convolution fusion | flops 618920448 | bytes 24397824 | tf_op jit(solution)/shard_map/while/body/eval_jaxpr/dot_general | solution.py:19
  184.1 1.5 fusion.12
  185.6 8.0 %fusion.3 = bf16[1536,1536]{0,1:T(8,128)(2,1)} fusion(bf16[1536,1536]{0,1:T(8,128)(2,1)S(1)} %get-tuple-element.57, f32[1536,1536]{1,0:T(8,128)} %get-tuple-element.62, f32[1536]{0:T(1024)S(1)} %get-tuple-element.56), kind=kLoop, calls=%fused_computation.6 | loop fusion | flops 11796480 | bytes 18880512 | tf_op jit(solution)/shard_map/while/body/eval_jaxpr/convert_element_type | solution.py:53
  193.6 0.0 copy-done.1
  193.6 2.4 fusion.9
  196.0 0.0 copy-done.9
  196.0 0.0 copy-done.10
  196.1 4.5 convolution_convert_fusion
  200.6 1.2 copy.29
  201.8 0.0 copy-start.3
  201.8 0.0 copy-start.4
  201.8 4.1 fusion.28
  205.9 0.0 copy-done.3
  205.9 0.0 copy-done.4
  206.0 0.0 copy-start.2
  206.0 1.0 fusion.29
  207.0 0.2 copy-done.2
  207.2 3.7 add_add_fusion
  210.9 0.0 reduce-scatter.3.cloned.1.call-update
  210.9 0.0 reduce-scatter.5.cloned.1.call-start
  211.0 7.3 %convolution_bitcast_fusion = f32[4096,768]{0,1:T(8,128)} fusion(bf16[384,4096]{1,0:T(8,128)(2,1)S(1)} %copy-done, bf16[384,128]{0,1:T(8,128)(2,1)} %fusion.12, bf16[384,128]{0,1:T(8,128)(2,1)} %fusion.9, bf16[384,512]{0,1:T(8,128)(2,1)S(1)} %bitcast.57), kind=kOutput, calls=%fused_computation.11 | convolution fusion | flops 2417688576 | bytes 16318464 | tf_op jit(solution)/shard_map/dot_general | solution.py:25
  218.2 0.0 reduce-scatter.5.cloned.1.call-update
  218.3 0.9 copy-done.8
  219.1 0.1 copy-done.12
  219.3 3.8 convolution_convert_fusion.1
  223.0 0.3 copy.26
  223.3 0.8 copy.36
  224.1 88.3 %reduce-scatter.3.cloned.1.call-done = f32[384,512]{1,0:T(8,128)} async-done(((f32[384,4096]{1,0:T(8,128)}), f32[384,512]{1,0:T(8,128)}) %reduce-scatter.3.cloned.1.call-update) | async-done | bytes 786448 | tf_op jit(solution)/shard_map/reduce_scatter | solution.py:103
  312.5 1.9 convert_element_type.51
  314.4 138.2 %reduce-scatter.5.cloned.1.call-done = f32[128,768]{0,1:T(8,128)} async-done(((f32[4096,768]{0,1:T(8,128)}), f32[128,768]{0,1:T(8,128)}) %reduce-scatter.5.cloned.1.call-update) | async-done | bytes 393232 | tf_op jit(solution)/shard_map/reduce_scatter | solution.py:108
  452.6 1.0 broadcast_multiply_fusion
  453.7 0.8 copy.30
  454.5 0.7 copy.32
  455.2 0.7 copy.31
  (12 shorter events, 0.1 us)
Async XLA Ops:
  7.2 89.7 %copy-start = (bf16[384,4096]{1,0:T(8,128)(2,1)S(1)}, bf16[384,4096]{1,0:T(8,128)(2,1)}, u32[]{:S(2)}) copy-start(bf16[384,4096]{1,0:T(8,128)(2,1)} %param.8) | copy-start | bytes 9437188
  10.7 157.6 %all-to-all-start = ((bf16[32,128,512]{2,1,0:T(8,128)(2,1)}), bf16[32,128,512]{2,1,0:T(8,128)(2,1)}, u32[]{:S(2)}, u32[]{:S(2)}) async-start(bf16[32,128,512]{2,1,0:T(8,128)(2,1)} %stack.2), calls=%async_computation | async-start | bytes 8388608 | tf_op jit(solution)/shard_map/all_to_all | solution.py:14
  20.6 76.3 %all-gather.5.cloned.1.call-start = ((), (), s32[]{:S(2)}) async-start(), calls=%async_computation.4 | async-start | bytes 1081344 | tf_op jit(solution)/shard_map/all_gather | solution.py:75
  21.3 144.1 %all-gather.3.cloned.1.call-start = ((), (), s32[]{:S(2)}) async-start(), calls=%async_computation.3 | async-start | bytes 1081344 | tf_op jit(solution)/shard_map/all_gather | solution.py:74
  22.1 290.4 %reduce-scatter.3.cloned.1.call-start = ((), (), s32[]{:S(2)}) async-start(), calls=%async_computation.5 | async-start | bytes 7077888 | tf_op jit(solution)/shard_map/reduce_scatter | solution.py:103
  177.7 1.4 copy-start.6
  177.7 1.4 copy-start.7
  177.7 1.4 copy-start.11
  184.1 9.5 %copy-start.1 = (bf16[1536,1536]{0,1:T(8,128)(2,1)}, bf16[1536,1536]{0,1:T(8,128)(2,1)S(1)}, u32[]{:S(2)}) copy-start(bf16[1536,1536]{0,1:T(8,128)(2,1)S(1)} %get-tuple-element.57) | copy-start | bytes 14155780
  185.6 10.4 %copy-start.9 = (bf16[384,128]{1,0:T(8,128)(2,1)S(1)}, bf16[384,128]{1,0:T(8,128)(2,1)}, u32[]{:S(2)}) copy-start(bf16[384,128]{1,0:T(8,128)(2,1)} %convolution_convert_fusion.4) | copy-start | bytes 294916
  185.6 10.4 %copy-start.10 = (bf16[1,1152,128]{2,1,0:T(8,128)(2,1)S(1)}, bf16[1,1152,128]{2,1,0:T(8,128)(2,1)}, u32[]{:S(2)}) copy-start(bf16[1,1152,128]{2,1,0:T(8,128)(2,1)} %param.13) | copy-start | bytes 884740
  201.8 4.2 copy-start.3
  201.8 4.2 copy-start.4
  206.0 1.2 copy-start.2
  206.0 1.2 copy-start.5
  210.9 241.7 %reduce-scatter.5.cloned.1.call-start = ((), (), s32[]{:S(2)}) async-start(), calls=%async_computation.6 | async-start | bytes 12976128 | tf_op jit(solution)/shard_map/reduce_scatter | solution.py:108
  218.2 0.9 copy-start.8
  218.2 1.0 copy-start.12
Sparse Core Ops, SparseCore 0:
  23.2 73.5 all-gather.4
  98.7 66.6 all-gather.2
  211.0 101.3 reduce-scatter.2
  314.9 137.6 reduce-scatter.4
